TPU v7x, 256 devices: a whole 4x4x8 slice. The times are simulated.
256 devices in a mesh: group: 8 (over x, core), inner: 32 (over z, y).
Axes of the slice: x: 4, y: 4, z: 8, core: 2. Of those that a mesh axis runs over, the one named last changes fastest.
Arguments:
- flow_field: float32 [1536, 1536, 128], P('inner', 'group'), may hold values from -6 to 6
- sketch_rows: float32 [1536, 128], P('inner'), may hold values from -6 to 6
- sketch_cols: float32 [1536, 128], P('group'), may hold values from -6 to 6
- sketch_depth: float32 [128, 128], replicated, may hold values from -6 to 6
- bit_widths: int32 [2], replicated, may hold values from 6 to 8
- bin_edges: int32 [9], replicated, may hold values from -6 to 6, as said below
Outputs:
- basis_one: float32 [1536, 128], P('inner')
- basis_two: float32 [1536, 128], P('group')
- core: float32 [128, 128, 128], P('inner', 'group')
- residual: float32 [2, 128, 128, 128], P(None, 'inner', 'group')
- energy: float32 [2, 1536, 128], P(None, 'inner')
- histogram: float32 [2, 1536, 8], P(None, 'inner')
Inputs may be any that keep to these rules, and one draw needn't show every extreme that they name: `bin_edges`: strictly increasing; the first is -6 and the last 6.
All inputs are finite; a program needn't handle non-finite values.
Results may differ from a plain program's by a relative error of at most 0.0008.
Values sent between devices are 32-bit elements; how exact they have to be, the bound alone decides.
No kernel may reach another device: no remote copies, remote signals or barrier semaphores. Data moves between devices by JAX's collectives and lax.ppermute only.
A program may use at most 128 MiB of HBM per device.

v0:
```python
import math
import jax
import jax.numpy as jnp
from jax import lax
from jax.sharding import PartitionSpec as P

N1 = 1536
N2 = 1536
N3 = 128
R = 128
NEDGE = 9
NBINS = 8
precise = lax.Precision.HIGHEST
two_pi = 2.0 * 3.141592653589793
error_boost = 16.0


def gram_of(sketch):
    return jnp.dot(sketch.T, sketch, precision=precise)


def orthonormal_rows(sketch, gram_matrix):
    lower_factor = jnp.linalg.cholesky(gram_matrix)
    return jax.scipy.linalg.solve_triangular(lower_factor, sketch.T, lower=True).T


def soft_residual(core_values, step_size):
    return -jnp.sin(two_pi * core_values[None] / step_size[:, None, None, None]) / two_pi


def local(flow_field, sketch_rows, sketch_cols, sketch_depth, bit_widths, bin_edges):
    reduced = jnp.einsum("ijk,kr->ijr", flow_field, sketch_depth, precision=precise)
    mode_one = jnp.einsum("ijr,jr->ir", reduced, sketch_cols, precision=precise)
    mode_two = jnp.einsum("ijr,ir->jr", reduced, sketch_rows, precision=precise)
    mode_one = lax.psum(mode_one, "group")
    basis_one = orthonormal_rows(mode_one, lax.psum(gram_of(mode_one), "inner"))
    mode_two = lax.psum(mode_two, "inner")
    basis_two = orthonormal_rows(mode_two, lax.psum(gram_of(mode_two), "group"))
    along_two = jnp.einsum("ijk,js->isk", flow_field, basis_two, precision=precise)
    levels = jnp.exp2(bit_widths.astype(jnp.float32) - 1.0) - 1.0
    summed_two = lax.psum_scatter(along_two, "group", scatter_dimension=1, tiled=True)
    partial_rows = jnp.einsum("ir,isk->rsk", basis_one, summed_two, precision=precise)
    core_shard = lax.psum_scatter(partial_rows, "inner", scatter_dimension=0, tiled=True)
    peak = lax.pmax(jnp.max(jnp.abs(core_shard)), ("group", "inner"))
    residual_shard = soft_residual(core_shard, peak / levels)
    spread = lax.all_gather(residual_shard, "group", axis=2, tiled=True)
    mixed_core = jnp.einsum(
        "ir,brsk->bisk",
        basis_one,
        lax.all_gather(spread, "inner", axis=1, tiled=True),
        precision=precise,
    )
    error_scale = error_boost * math.sqrt(N1 * N2) / R
    field_error = error_scale * jnp.einsum(
        "bisk,js->bijk", mixed_core, basis_two, precision=precise
    )
    energy_part = jnp.sum(field_error * field_error, axis=2) / N2
    edge_values = bin_edges.astype(jnp.float32)
    ramp_part = jnp.stack(
        [
            jnp.sum(jnp.clip(field_error - edge_values[index_edge] + 0.5, 0.0, 1.0), axis=(2, 3))
            for index_edge in range(NEDGE)
        ],
        axis=-1,
    )
    energy, ramp_sums = lax.psum((energy_part, ramp_part), "group")
    histogram = (ramp_sums[..., :-1] - ramp_sums[..., 1:]) * (NBINS / (N2 * N3))
    return (basis_one, basis_two, core_shard, residual_shard, energy, histogram)


def solution(mesh):
    in_specs = (P("inner", "group", None), P("inner", None), P("group", None), P(), P(), P())
    out_specs = (
        P("inner", None),
        P("group", None),
        P("inner", "group", None),
        P(None, "inner", "group", None),
        P(None, "inner", None),
        P(None, "inner", None),
    )
    return jax.shard_map(local, mesh=mesh, in_specs=in_specs, out_specs=out_specs, check_vma=False)
```

profile of v0, /device:TPU:8, one launch (start us, length us, event | category | flops | bytes accessed | tf_op | source)
XLA Modules:
  0.0 863.6 jit_solution(15359649875850458368)
XLA Ops:
  8.0 7.1 multiply_reduce_fusion.2
  15.2 26.1 %psum.42 = f32[48,128]{0,1:T(8,128)S(1)} all-reduce(f32[48,128]{0,1:T(8,128)S(1)} %bitcast.98), channel_id=1, replica_groups=mesh['group'=8,'inner'=32] {'group'}, use_global_device_ids=true, to_apply=%region_0.0 | all-reduce | flops 6144 | bytes 49152 | tf_op jit(solution)/shard_map/psum | solution.py:35
  42.2 2.8 multiply_reduce_fusion.1
  45.8 143.9 %all-reduce.7.cloned.1.call-done = (f32[128,128]{0,1:T(8,128)}, f32[192,128]{0,1:T(8,128)}) async-done(((f32[128,128]{0,1:T(8,128)}, f32[192,128]{0,1:T(8,128)}), (f32[128,128]{0,1:T(8,128)}, f32[192,128]{0,1:T(8,128)})) %all-reduce.7.cloned.1.call-update) | async-done | bytes 163856 | tf_op jit(solution)/shard_map/psum | solution.py:36
  189.7 1.9 fusion.26
  191.8 64.2 %all-reduce.5.cloned.1.call-done = f32[128,128]{0,1:T(8,128)} async-done(((f32[128,128]{0,1:T(8,128)}), f32[128,128]{0,1:T(8,128)}) %all-reduce.5.cloned.1.call-update) | async-done | bytes 65552 | tf_op jit(solution)/shard_map/psum | solution.py:38
  257.8 11.7 %cholesky.55 = f32[128,128]{1,0:T(8,128)S(1)} custom-call(f32[128,128]{1,0:T(8,128)S(1)} %fusion.14), custom_call_target="Cholesky" | custom-call | tf_op jit(solution)/shard_map/jit(cholesky)/cholesky | solution.py:23
  270.8 9.8 %custom-call.11 = f32[1,128,128]{1,2,0:T(8,128)S(1)} custom-call(f32[1,128,128]{2,1,0:T(8,128)S(1)} %fusion.11), custom_call_target="InvertDiagBlocksLowerTriangular" | custom-call | tf_op jit(solution)/shard_map/jit(_solve_triangular)/triangular_solve | solution.py:24
  280.6 1.3 fusion.12
  281.9 4.8 fusion.6
  286.8 3.5 copy.57
  290.7 11.7 %cholesky.44 = f32[128,128]{1,0:T(8,128)S(1)} custom-call(f32[128,128]{1,0:T(8,128)S(1)} %fusion.17), custom_call_target="Cholesky" | custom-call | tf_op jit(solution)/shard_map/jit(cholesky)/cholesky | solution.py:23
  303.8 9.8 %custom-call.10 = f32[1,128,128]{1,2,0:T(8,128)S(1)} custom-call(f32[1,128,128]{2,1,0:T(8,128)S(1)} %fusion.10), custom_call_target="InvertDiagBlocksLowerTriangular" | custom-call | tf_op jit(solution)/shard_map/jit(_solve_triangular)/triangular_solve | solution.py:24
  313.9 14.2 %reduce-scatter.3.cloned.1.call-done = f32[48,16,128]{2,0,1:T(8,128)} async-done(((f32[48,128,128]{2,0,1:T(8,128)}), f32[48,16,128]{2,0,1:T(8,128)}) %reduce-scatter.3.cloned.1.call-update) | async-done | bytes 393232 | tf_op jit(solution)/shard_map/reduce_scatter | solution.py:41
  328.1 2.0 fusion.21
  330.1 1.6 copy.23
  331.8 215.3 %reduce-scatter.5.cloned.1.call-done = f32[4,16,128]{2,1,0:T(8,128)} async-done(((f32[128,16,128]{2,1,0:T(8,128)}), f32[4,16,128]{2,1,0:T(8,128)}) %reduce-scatter.5.cloned.1.call-update) | async-done | bytes 32784 | tf_op jit(solution)/shard_map/reduce_scatter | solution.py:43
  547.1 1.4 broadcast_multiply_fusion.2
  548.5 74.3 %pmax.7 = f32[]{:T(128)} all-reduce(f32[]{:T(128)} %get-tuple-element.34), channel_id=1, replica_groups=mesh['group'=8,'inner'=32] {'group','inner'}, use_global_device_ids=true, to_apply=%region_9.11 | all-reduce | flops 1 | bytes 8 | tf_op jit(solution)/shard_map/pmax | solution.py:44
  623.8 14.5 %all_gather.6 = f32[2,4,128,128]{3,2,1,0:T(8,128)} all-gather(f32[2,4,16,128]{3,2,1,0:T(8,128)S(1)} %fusion.9), channel_id=1, replica_groups=mesh['group'=8,'inner'=32] {'group'}, dimensions={2}, use_global_device_ids=true | all-gather | bytes 589824 | tf_op jit(solution)/shard_map/all_gather | solution.py:46
  639.0 135.6 %all-gather.2.cloned.1.call-done = f32[2,128,128,128]{3,2,1,0:T(8,128)} async-done(((f32[2,4,128,128]{3,2,1,0:T(8,128)}), f32[2,128,128,128]{3,2,1,0:T(8,128)}) %all-gather.2.cloned.1.call-update) | async-done | bytes 16777232 | tf_op jit(solution)/shard_map/all_gather | solution.py:50
  774.6 22.9 %fusion = f32[2,128,128,48]{2,3,1,0:T(8,128)S(1)} fusion(f32[2,128,128,128]{3,2,1,0:T(8,128)} %all-gather.2.cloned.1.call-done, f32[128,48]{0,1:T(8,128)S(1)} %fusion.15), kind=kOutput, calls=%fused_computation | convolution fusion | flops 2415919104 | bytes 23093248 | tf_op jit(solution)/shard_map/ir,brsk->bisk/dot_general | solution.py:47
  797.5 32.9 %clamp_reduce_fusion = (f32[2,48]{1,0:T(2,128)S(1)}, f32[2,48]{1,0:T(2,128)S(1)}, f32[2,48]{1,0:T(2,128)S(1)}, f32[2,48]{1,0:T(2,128)S(1)}, f32[2,48]{1,0:T(2,12...) fusion(f32[]{:T(128)} %bitcast.39, f32[]{:T(128)} %bitcast.23, ...), kind=kOutput, calls=%fused_computation.2 | convolution fusion | flops 3715877888 | bytes 6442404 | tf_op jit(solution)/shard_map/bisk,js->bijk/dot_general | solution.py:54
  830.6 25.9 %all-reduce.1 = (f32[2,48,128]{2,1,0:T(8,128)}, f32[2,48,9]{1,0,2:T(2,128)S(1)}) all-reduce(f32[2,48,128]{2,1,0:T(8,128)S(1)} %broadcast_multiply_fusion.1, f32[2,48,9]{1,0,2:T(2,128)S(1)} %constant_dynamic-update-slice_fusion), channel_id=1, replica_groups=mesh['group'=8,'inner'=32] {'group'}, use_global_device_ids=true, to_apply=%region_11.13 | all-reduce | flops 13152 | bytes 105216 | tf_op jit(solution)/shard_map/psum | solution.py:66
  (56 shorter events, 10.4 us)
Async XLA Ops:
  7.2 0.8 copy-start
  7.2 35.0 %copy-start.5 = (f32[48,128]{1,0:T(8,128)S(1)}, f32[48,128]{1,0:T(8,128)}, u32[]{:S(2)}) copy-start(f32[48,128]{1,0:T(8,128)} %param.8) | copy-start | bytes 73732
  7.2 182.5 %all-reduce.7.cloned.1.call-start = ((), (), s32[]{:S(2)}) async-start(), calls=%async_computation.6 | async-start | bytes 393216 | tf_op jit(solution)/shard_map/psum | solution.py:36
  45.7 210.2 %all-reduce.5.cloned.1.call-start = ((), (), s32[]{:S(2)}) async-start(), calls=%async_computation.2 | async-start | bytes 131072 | tf_op jit(solution)/shard_map/psum | solution.py:38
  189.7 100.9 %copy-start.3 = (f32[128,128]{0,1:T(8,128)S(1)}, f32[128,128]{0,1:T(8,128)}, u32[]{:S(2)}) copy-start(f32[128,128]{0,1:T(8,128)} %get-tuple-element.29) | copy-start | bytes 196612
  191.6 136.5 %reduce-scatter.3.cloned.1.call-start = ((), (), s32[]{:S(2)}) async-start(), calls=%async_computation.3 | async-start | bytes 3538944 | tf_op jit(solution)/shard_map/reduce_scatter | solution.py:41
  281.9 515.6 %copy-start.1 = (f32[128,192]{0,1:T(8,128)}, f32[128,192]{0,1:T(8,128)S(1)}, u32[]{:S(2)}) copy-start(f32[128,192]{0,1:T(8,128)S(1)} %fusion.12) | copy-start | bytes 294916
  281.9 340.9 %copy-start.6 = (s32[2]{0:T(128)S(1)}, s32[2]{0:T(128)}, u32[]{:S(2)}) copy-start(s32[2]{0:T(128)} %param.11) | copy-start | bytes 28
  286.8 351.5 %copy-start.7 = (s32[9]{0:T(128)S(1)}, s32[9]{0:T(128)}, u32[]{:S(2)}) copy-start(s32[9]{0:T(128)} %param.12) | copy-start | bytes 112
  290.3 256.8 %reduce-scatter.5.cloned.1.call-start = ((), (), s32[]{:S(2)}) async-start(), calls=%async_computation.4 | async-start | bytes 1081344 | tf_op jit(solution)/shard_map/reduce_scatter | solution.py:43
  313.9 483.7 %copy-start.4 = (f32[128,48]{0,1:T(8,128)}, f32[128,48]{0,1:T(8,128)S(1)}, u32[]{:S(2)}) copy-start(f32[128,48]{0,1:T(8,128)S(1)} %fusion.15) | copy-start | bytes 73732
  331.7 442.9 %all-gather.2.cloned.1.call-start = ((), (), s32[]{:S(2)}) async-start(), calls=%async_computation.5 | async-start | bytes 17301504 | tf_op jit(solution)/shard_map/all_gather | solution.py:50
  623.8 173.7 %copy-start.2 = (f32[2,4,16,128]{3,2,1,0:T(8,128)}, f32[2,4,16,128]{3,2,1,0:T(8,128)S(1)}, u32[]{:S(2)}) copy-start(f32[2,4,16,128]{3,2,1,0:T(8,128)S(1)} %fusion.9) | copy-start | bytes 196612
Sparse Core Ops, SparseCore 0:
  45.9 143.7 all-reduce.6
  192.5 63.3 all-reduce.4
  290.4 37.5 reduce-scatter.2
  332.3 214.7 reduce-scatter.4
  638.4 136.1 all-gather.1
where the time goes:
time: 864 us
  waiting for transfers between devices  573 us (66%)
  blocking collectives  141 us (16%)
  matrix products  74.1 us (9%)
  other arithmetic  51.7 us (6%)
  between operations  14 us (2%)
  local copies, waits for them, and re-layouts  9.15 us (1%)
    reduce_scatter x1, waiting for transfers between devices, local(): lax.psum_scatter(partial_rows, 'inner', scatter_dimension=0, tiled=True)  215 us
    psum x1, waiting for transfers between devices, local(): basis_one = orthonormal_rows(mode_one, lax.psum(gram_of(mode_one), 'inner'))  144 us
    all_gather x1, waiting for transfers between devices, local(): lax.all_gather(spread, 'inner', axis=1, tiled=True)  136 us
    pmax x1, blocking collectives, local(): peak = lax.pmax(jnp.max(jnp.abs(core_shard)), ('group', 'inner'))  74.3 us
    psum x1, waiting for transfers between devices, local(): basis_two = orthonormal_rows(mode_two, lax.psum(gram_of(mode_two), 'group'))  64.2 us
    dot_general x1, matrix products, local(): jnp.einsum('bisk,js->bijk', mixed_core, basis_two, precision=precise)  32.9 us
    psum x1, blocking collectives, local(): mode_one = lax.psum(mode_one, 'group')  26.1 us
    psum x1, blocking collectives, local(): energy, ramp_sums = lax.psum((energy_part, ramp_part), 'group')  25.9 us
  transfers between devices with their start and end apart: 5, of which 5 were waited for; matrix products, arithmetic and copies ran while one was open for 3% of the time, Pallas kernels for 0%

commit v1 on v0

--- a/solution.py
+++ b/solution.py
@@ -47,7 +47,9 @@
     mixed_core = jnp.einsum(
         "ir,brsk->bisk",
         basis_one,
-        lax.all_gather(spread, "inner", axis=1, tiled=True),
+        jnp.concatenate(
+            lax.all_to_all(jnp.stack([spread] * lax.axis_size("inner")), "inner", 0, 0), axis=1
+        ),
         precision=precise,
     )
     error_scale = error_boost * math.sqrt(N1 * N2) / R

time: 864 us -> 1150 us (1.33)
  the two profiles are of different devices: /device:TPU:8 before, /device:TPU:16 now
where the time goes in v1:
time: 1150 us
  waiting for transfers between devices  841 us (73%)
  blocking collectives  137 us (12%)
  matrix products  72.9 us (6%)
  other arithmetic  51.7 us (4%)
  local copies, waits for them, and re-layouts  20.3 us (2%)
  between operations  14.5 us (1%)
    all_to_all x1, waiting for transfers between devices, local(): lax.all_to_all(jnp.stack([spread] * lax.axis_size('inner')), 'inner', 0, 0)  404 us
    reduce_scatter x1, waiting for transfers between devices, local(): lax.psum_scatter(partial_rows, 'inner', scatter_dimension=0, tiled=True)  215 us
    psum x1, waiting for transfers between devices, local(): basis_one = orthonormal_rows(mode_one, lax.psum(gram_of(mode_one), 'inner'))  144 us
    pmax x1, blocking collectives, local(): peak = lax.pmax(jnp.max(jnp.abs(core_shard)), ('group', 'inner'))  73.7 us
    psum x1, waiting for transfers between devices, local(): basis_two = orthonormal_rows(mode_two, lax.psum(gram_of(mode_two), 'group'))  64.1 us
    dot_general x1, matrix products, local(): jnp.einsum('bisk,js->bijk', mixed_core, basis_two, precision=precise)  32.9 us
    psum x1, blocking collectives, local(): mode_one = lax.psum(mode_one, 'group')  26.1 us
    another operation x6, other arithmetic, orthonormal_rows(): lower_factor = jnp.linalg.cholesky(gram_matrix)  24.8 us
  transfers between devices with their start and end apart: 5, of which 5 were waited for; matrix products, arithmetic and copies ran while one was open for 2% of the time, Pallas kernels for 0%

profile of v1, /device:TPU:16, one launch (start us, length us, event | category | flops | bytes accessed | tf_op | source)
XLA Modules:
  0.0 1147.9 jit_solution(17126635183540514190)
XLA Ops:
  8.0 7.1 multiply_reduce_fusion.2
  15.2 26.1 %psum.42 = f32[48,128]{0,1:T(8,128)S(1)} all-reduce(f32[48,128]{0,1:T(8,128)S(1)} %bitcast.96), channel_id=1, replica_groups=mesh['group'=8,'inner'=32] {'group'}, use_global_device_ids=true, to_apply=%region_0.0 | all-reduce | flops 6144 | bytes 49152 | tf_op jit(solution)/shard_map/psum | solution.py:35
  42.2 2.8 multiply_reduce_fusion.1
  45.8 143.5 %all-reduce.7.cloned.1.call-done = (f32[128,128]{0,1:T(8,128)}, f32[192,128]{0,1:T(8,128)}) async-done(((f32[128,128]{0,1:T(8,128)}, f32[192,128]{0,1:T(8,128)}), (f32[128,128]{0,1:T(8,128)}, f32[192,128]{0,1:T(8,128)})) %all-reduce.7.cloned.1.call-update) | async-done | bytes 163856 | tf_op jit(solution)/shard_map/psum | solution.py:36
  189.3 1.9 fusion.28
  191.8 64.1 %all-reduce.5.cloned.1.call-done = f32[128,128]{0,1:T(8,128)} async-done(((f32[128,128]{0,1:T(8,128)}), f32[128,128]{0,1:T(8,128)}) %all-reduce.5.cloned.1.call-update) | async-done | bytes 65552 | tf_op jit(solution)/shard_map/psum | solution.py:38
  257.7 11.7 %cholesky.55 = f32[128,128]{1,0:T(8,128)S(1)} custom-call(f32[128,128]{1,0:T(8,128)S(1)} %fusion.17), custom_call_target="Cholesky" | custom-call | tf_op jit(solution)/shard_map/jit(cholesky)/cholesky | solution.py:23
  270.8 9.8 custom-call.11
  281.9 7.0 convolution_bitcast_fusion
  289.2 11.7 %cholesky.44 = f32[128,128]{1,0:T(8,128)S(1)} custom-call(f32[128,128]{1,0:T(8,128)S(1)} %fusion.20), custom_call_target="Cholesky" | custom-call | tf_op jit(solution)/shard_map/jit(cholesky)/cholesky | solution.py:23
  302.3 9.8 custom-call.10
  312.4 14.3 %reduce-scatter.3.cloned.1.call-done = f32[48,16,128]{2,1,0:T(8,128)} async-done(((f32[48,128,128]{2,1,0:T(8,128)}), f32[48,16,128]{2,1,0:T(8,128)}) %reduce-scatter.3.cloned.1.call-update) | async-done | bytes 393232 | tf_op jit(solution)/shard_map/reduce_scatter | solution.py:41
  326.7 2.0 fusion.7
  328.8 1.6 copy.31
  330.4 215.2 %reduce-scatter.5.cloned.1.call-done = f32[4,16,128]{2,1,0:T(8,128)} async-done(((f32[128,16,128]{2,1,0:T(8,128)}), f32[4,16,128]{2,1,0:T(8,128)}) %reduce-scatter.5.cloned.1.call-update) | async-done | bytes 32784 | tf_op jit(solution)/shard_map/reduce_scatter | solution.py:43
  547.0 73.7 %pmax.7 = f32[]{:T(128)} all-reduce(f32[]{:T(128)} %get-tuple-element.40), channel_id=1, replica_groups=mesh['group'=8,'inner'=32] {'group','inner'}, use_global_device_ids=true, to_apply=%region_9.11 | all-reduce | flops 1 | bytes 8 | tf_op jit(solution)/shard_map/pmax | solution.py:44
  621.6 13.1 %all_gather.3 = f32[2,4,128,128]{3,2,1,0:T(8,128)S(1)} all-gather(f32[2,4,16,128]{3,2,1,0:T(8,128)S(1)} %fusion.12), channel_id=1, replica_groups=mesh['group'=8,'inner'=32] {'group'}, dimensions={2}, use_global_device_ids=true | all-gather | bytes 589824 | tf_op jit(solution)/shard_map/all_gather | solution.py:46
  634.7 7.8 stack.22
  642.6 8.7 all-to-all-start
  652.0 404.3 %all-to-all-done = f32[32,2,4,128,128]{4,3,2,1,0:T(8,128)} async-done(((f32[32,2,4,128,128]{4,3,2,1,0:T(8,128)}), f32[32,2,4,128,128]{4,3,2,1,0:T(8,128)}, u32[]{:S(2)}, u32[]{:S(2)}) %all-to-all-start) | async-done | bytes 16777248 | tf_op jit(solution)/shard_map/all_to_all | solution.py:51
  1056.3 6.8 copy.32
  1063.1 19.6 %fusion.4 = f32[2,48,128,128]{3,1,2,0:T(8,128)S(1)} fusion(f32[2,128,128,128]{3,2,1,0:T(8,128)S(1)} %bitcast.93, f32[128,48]{0,1:T(8,128)S(1)} %fusion.18), kind=kOutput, calls=%fused_computation.17 | convolution fusion | flops 2415919104 | bytes 23093248 | tf_op jit(solution)/shard_map/ir,brsk->bisk/dot_general | solution.py:47
  1082.7 32.9 %clamp_reduce_fusion = (f32[2,48]{1,0:T(2,128)S(1)}, f32[2,48]{1,0:T(2,128)S(1)}, f32[2,48]{1,0:T(2,128)S(1)}, f32[2,48]{1,0:T(2,128)S(1)}, f32[2,48]{1,0:T(2,12...) fusion(f32[]{:T(128)} %bitcast.41, f32[]{:T(128)} %bitcast.25, ...), kind=kOutput, calls=%fused_computation.2 | convolution fusion | flops 3715877888 | bytes 6442404 | tf_op jit(solution)/shard_map/bisk,js->bijk/dot_general | solution.py:56
  1115.7 24.6 %all-reduce.1 = (f32[2,48,128]{2,1,0:T(8,128)}, f32[2,48,9]{1,0,2:T(2,128)S(1)}) all-reduce(f32[2,48,128]{2,1,0:T(8,128)S(1)} %broadcast_multiply_fusion.1, f32[2,48,9]{1,0,2:T(2,128)S(1)} %constant_dynamic-update-slice_fusion), channel_id=1, replica_groups=mesh['group'=8,'inner'=32] {'group'}, use_global_device_ids=true, to_apply=%region_11.13 | all-reduce | flops 13152 | bytes 105216 | tf_op jit(solution)/shard_map/psum | solution.py:68
  (58 shorter events, 13.3 us)
Async XLA Ops:
  7.2 0.8 copy-start
  7.2 35.0 %copy-start.6 = (f32[48,128]{1,0:T(8,128)S(1)}, f32[48,128]{1,0:T(8,128)}, u32[]{:S(2)}) copy-start(f32[48,128]{1,0:T(8,128)} %param.8) | copy-start | bytes 73732
  7.2 182.1 %all-reduce.7.cloned.1.call-start = ((), (), s32[]{:S(2)}) async-start(), calls=%async_computation.6 | async-start | bytes 393216 | tf_op jit(solution)/shard_map/psum | solution.py:36
  45.0 575.7 %copy-start.7 = (s32[2]{0:T(128)S(1)}, s32[2]{0:T(128)}, u32[]{:S(2)}) copy-start(s32[2]{0:T(128)} %param.11) | copy-start | bytes 28
  45.7 210.2 %all-reduce.5.cloned.1.call-start = ((), (), s32[]{:S(2)}) async-start(), calls=%async_computation.3 | async-start | bytes 131072 | tf_op jit(solution)/shard_map/psum | solution.py:38
  189.3 99.8 %copy-start.4 = (f32[128,128]{0,1:T(8,128)S(1)}, f32[128,128]{0,1:T(8,128)}, u32[]{:S(2)}) copy-start(f32[128,128]{0,1:T(8,128)} %get-tuple-element.35) | copy-start | bytes 196612
  191.2 135.5 %reduce-scatter.3.cloned.1.call-start = ((), (), s32[]{:S(2)}) async-start(), calls=%async_computation.4 | async-start | bytes 3538944 | tf_op jit(solution)/shard_map/reduce_scatter | solution.py:41
  281.8 800.8 %copy-start.2 = (f32[128,192]{0,1:T(8,128)}, f32[128,192]{0,1:T(8,128)S(1)}, u32[]{:S(2)}) copy-start(f32[128,192]{0,1:T(8,128)S(1)} %fusion.15) | copy-start | bytes 294916
  288.9 256.7 %reduce-scatter.5.cloned.1.call-start = ((), (), s32[]{:S(2)}) async-start(), calls=%async_computation.5 | async-start | bytes 1081344 | tf_op jit(solution)/shard_map/reduce_scatter | solution.py:43
  312.4 750.7 %copy-start.5 = (f32[128,48]{0,1:T(8,128)}, f32[128,48]{0,1:T(8,128)S(1)}, u32[]{:S(2)}) copy-start(f32[128,48]{0,1:T(8,128)S(1)} %fusion.18) | copy-start | bytes 73732
  621.6 21.0 %copy-start.3 = (f32[2,4,16,128]{3,2,1,0:T(8,128)}, f32[2,4,16,128]{3,2,1,0:T(8,128)S(1)}, u32[]{:S(2)}) copy-start(f32[2,4,16,128]{3,2,1,0:T(8,128)S(1)} %fusion.12) | copy-start | bytes 196612
  642.6 8.7 copy-start.8
  642.6 413.7 %all-to-all-start = ((f32[32,2,4,128,128]{4,3,2,1,0:T(8,128)}), f32[32,2,4,128,128]{4,3,2,1,0:T(8,128)}, u32[]{:S(2)}, u32[]{:S(2)}) async-start(f32[32,2,4,128,128]{4,3,2,1,0:T(8,128)} %stack.22), calls=%async_computation.2 | async-start | bytes 33554432 | tf_op jit(solution)/shard_map/all_to_all | solution.py:51
  1082.7 58.2 %copy-start.1 = (f32[128,128]{1,0:T(8,128)S(1)}, f32[128,128]{1,0:T(8,128)}, u32[]{:S(2)}) copy-start(f32[128,128]{1,0:T(8,128)} %param.10) | copy-start | bytes 196612
Sparse Core Ops, SparseCore 0:
  45.9 143.3 all-reduce.6
  192.2 63.6 all-reduce.4
  289.0 37.6 reduce-scatter.2
  331.0 214.5 reduce-scatter.4
